TPU v7x, 256 devices: a whole 4x4x8 slice. The times are simulated.
256 devices in a mesh: seq: 64 (over z, y, core), head: 4 (over x).
Axes of the slice: x: 4, y: 4, z: 8, core: 2. Of those that a mesh axis runs over, the one named last changes fastest.
Arguments:
- query: bfloat16 [40960, 2048], P(('seq', 'head')), may hold values from -5 to 5
- key: bfloat16 [40960, 2048], P(('seq', 'head')), may hold values from -5 to 5
- value: bfloat16 [40960, 2048], P(('seq', 'head')), may hold values from -6 to 6
- grad_out: bfloat16 [40960, 2048], P(('seq', 'head')), may hold values from -6 to 6
- rand_blocks: int32 [640, 3], replicated, may hold values from 0 to 639, as said below
Outputs:
- grad_query: bfloat16 [40960, 2048], P(('seq', 'head'))
- grad_key: bfloat16 [40960, 2048], P(('seq', 'head'))
- grad_value: bfloat16 [40960, 2048], P(('seq', 'head'))
Inputs may be any that keep to these rules, and one draw needn't show every extreme that they name: `rand_blocks`: row j lists the 3 random key blocks of query block j. Block b lies on index b // 10 of seq. The blocks of one row lie on 3 different indices. No listed block lies on index 0 or on the index of the query block itself. The query blocks of one index of seq list at most 1 block lying on any one other index.
All inputs are finite; a program needn't handle non-finite values.
Results may differ from a plain program's by a relative error of at most 0.008.
Values may be sent and summed in bfloat16 or wider, within the bound.
No kernel may reach another device: no remote copies, remote signals or barrier semaphores. Data moves between devices by JAX's collectives and lax.ppermute only.
A program may use at most 384 MiB of HBM per device.

v0:
```python
import jax
import jax.numpy as jnp
from jax import lax
from jax.sharding import PartitionSpec as P

HD = 128
BLOCK = 64
G = 2
R = 3


big_negative = -1e30


def broadcast(block, axis, source):
    peers = lax.axis_size(axis)
    block = jnp.where(lax.axis_index(axis) == source, block, jnp.zeros_like(block))
    step = 1
    while step * 2 < peers:
        step *= 2
    while step >= 1:
        pairs = [(i, i + step) for i in range(0, peers, 2 * step) if i + step < peers]
        block = block + lax.ppermute(block, axis, pairs)
        step //= 2
    return block


def reduce_to_first(block, axis):
    peers = lax.axis_size(axis)
    step = 1
    while step < peers:
        pairs = [(i + step, i) for i in range(0, peers, 2 * step) if i + step < peers]
        block = block + lax.ppermute(block, axis, pairs)
        step *= 2
    return block


def extended_2(shard, sides, width):
    for axis, dim in sides:
        peers, length = (lax.axis_size(axis), shard.shape[dim])
        up = [(i, (i + 1) % peers) for i in range(peers - 1)]
        down = [(j, i) for i, j in up]
        last = lax.slice_in_dim(shard, length - width, length, axis=dim)
        leading = lax.slice_in_dim(shard, 0, width, axis=dim)
        before = lax.ppermute(last, axis, up)
        after = lax.ppermute(leading, axis, down)
        shard = jnp.concatenate([before, shard, after], axis=dim)
    return shard


def request_plan(requested, device, per_dev):
    wanted_row = requested[device]
    owners = wanted_row // per_dev
    within = wanted_row % per_dev
    usable = jnp.ones(wanted_row.shape, jnp.bool_)
    positions = jnp.arange(owners.shape[0])
    earlier = (owners[:, None] == owners[None, :]) & (positions[None, :] < positions[:, None])
    slot_rank = jnp.sum(earlier.astype(jnp.int32), axis=1)
    return (owners, within, slot_rank, usable)


def on_device(query, key, value, grad_out, rand_blocks):
    stacked = jnp.stack([query, key, value, grad_out])
    stacked = lax.all_to_all(stacked, "head", split_axis=2, concat_axis=1, tiled=True)
    queries, keys, values, out_grads = stacked[0], stacked[1], stacked[2], stacked[3]
    tokens, features = queries.shape
    head_count = features // HD
    per_dev = tokens // BLOCK
    seq_count = lax.axis_size("seq")
    device = lax.axis_index("seq")
    capacity = (per_dev * R + seq_count - 3) // (seq_count - 2)
    rand_count = per_dev * R
    score_scale = HD ** (-0.5)
    requested = rand_blocks.reshape(seq_count, rand_count)
    owners_all, within_all, rank_all, usable_all = jax.vmap(
        lambda sender: request_plan(requested, sender, per_dev)
    )(jnp.arange(seq_count, dtype=jnp.int32))
    to_me = usable_all & (owners_all == device)
    slot_ids = jnp.arange(capacity)
    block_ids = jnp.arange(per_dev)
    matches = (
        to_me[:, :, None, None]
        & (rank_all[:, :, None, None] == slot_ids[None, None, :, None])
        & (within_all[:, :, None, None] == block_ids[None, None, None, :])
    )
    chooser = jnp.sum(matches.astype(jnp.float32), axis=1)
    my_owners, my_within, my_rank, my_usable = request_plan(requested, device, per_dev)
    my_slot = jnp.clip(my_owners, 0, seq_count - 1) * capacity + my_rank
    own_pairs = jnp.stack([keys, values]).reshape(2, per_dev, BLOCK, features)
    served = jnp.einsum(
        "dcb,sbxf->dcsxf",
        chooser.astype(jnp.bfloat16),
        own_pairs,
        preferred_element_type=jnp.float32,
    ).astype(jnp.bfloat16)
    outgoing = served.reshape(seq_count * capacity, 2, BLOCK, features)
    leading = jnp.stack([keys[: G * BLOCK], values[: G * BLOCK]])
    global_pairs = broadcast(leading, "seq", 0).reshape(2, G, BLOCK, features)
    extended = extended_2(jnp.stack([keys, values]), (("seq", 1),), BLOCK)
    outgoing, global_pairs, extended = lax.optimization_barrier((outgoing, global_pairs, extended))
    incoming = lax.all_to_all(outgoing, "seq", split_axis=0, concat_axis=0, tiled=True)

    left_pair = extended[:, :BLOCK]
    right_pair = extended[:, -BLOCK:]
    framed = jnp.concatenate([left_pair[:, None], own_pairs, right_pair[:, None]], axis=1)
    window = jnp.stack(
        [framed[:, 0:per_dev], framed[:, 1 : per_dev + 1], framed[:, 2 : per_dev + 2]], axis=2
    )
    global_slots = jnp.broadcast_to(global_pairs[:, None], (2, per_dev, G, BLOCK, features))
    local = jnp.concatenate([window, global_slots], axis=2)
    local_count = 3 + G
    local_keys = local[0].reshape(per_dev, local_count, BLOCK, head_count, HD)
    local_values = local[1].reshape(per_dev, local_count, BLOCK, head_count, HD)
    block_index = device * per_dev + jnp.arange(per_dev)
    glob_index = jnp.arange(G)
    intersections = jnp.abs(glob_index[None, :] - block_index[:, None]) <= 1
    live_local = jnp.concatenate(
        [
            (block_index >= 1)[:, None],
            jnp.ones((per_dev, 1), jnp.bool_),
            (block_index <= seq_count * per_dev - 2)[:, None],
            jnp.logical_not(intersections),
        ],
        axis=1,
    )
    query_blocks = queries.reshape(per_dev, BLOCK, head_count, HD)
    dout_blocks = out_grads.reshape(per_dev, BLOCK, head_count, HD)
    scores_local = (
        jnp.einsum("bxhd,bkyhd->bhxky", query_blocks, local_keys, preferred_element_type=jnp.float32)
        * score_scale
    )
    scores_local = jnp.where(live_local[:, None, None, :, None], scores_local, big_negative)
    grads_local = jnp.einsum(
        "bxhd,bkyhd->bhxky", dout_blocks, local_values, preferred_element_type=jnp.float32
    )
    max_local = jnp.max(scores_local, axis=(3, 4), keepdims=True)

    fetched = incoming[my_slot]
    randoms = fetched.reshape(per_dev, R, 2, BLOCK, features)
    rand_keys = randoms[:, :, 0].reshape(per_dev, R, BLOCK, head_count, HD)
    rand_values = randoms[:, :, 1].reshape(per_dev, R, BLOCK, head_count, HD)
    scores_rand = (
        jnp.einsum("bxhd,bkyhd->bhxky", query_blocks, rand_keys, preferred_element_type=jnp.float32)
        * score_scale
    )
    grads_rand = jnp.einsum(
        "bxhd,bkyhd->bhxky", dout_blocks, rand_values, preferred_element_type=jnp.float32
    )
    row_max = jnp.maximum(max_local, jnp.max(scores_rand, axis=(3, 4), keepdims=True))
    weights_local = jnp.exp(scores_local - row_max)
    weights_rand = jnp.exp(scores_rand - row_max)
    row_total = jnp.sum(weights_local, axis=(3, 4), keepdims=True) + jnp.sum(
        weights_rand, axis=(3, 4), keepdims=True
    )
    probs_local = weights_local / row_total
    probs_rand = weights_rand / row_total
    row_dot = jnp.sum(probs_local * grads_local, axis=(3, 4), keepdims=True) + jnp.sum(
        probs_rand * grads_rand, axis=(3, 4), keepdims=True
    )
    dscores_rand = (probs_rand * (grads_rand - row_dot)).astype(jnp.bfloat16)
    low_rand = probs_rand.astype(jnp.bfloat16)
    key_rand = (
        jnp.einsum(
            "bhxky,bxhd->bkyhd", dscores_rand, query_blocks, preferred_element_type=jnp.float32
        )
        * score_scale
    )
    value_rand = jnp.einsum(
        "bhxky,bxhd->bkyhd", low_rand, dout_blocks, preferred_element_type=jnp.float32
    )
    rand_terms = (
        jnp.stack([key_rand, value_rand])
        .reshape(2, rand_count, BLOCK, features)
        .transpose(1, 0, 2, 3)
        .astype(jnp.bfloat16)
    )
    target = jnp.where(my_usable, my_slot, seq_count * capacity)
    placer = (target[:, None] == jnp.arange(seq_count * capacity)[None, :]).astype(jnp.bfloat16)
    outgoing_back = jnp.einsum(
        "js,jkxf->skxf", placer, rand_terms, preferred_element_type=jnp.float32
    ).astype(jnp.bfloat16)
    arrived = lax.all_to_all(outgoing_back, "seq", split_axis=0, concat_axis=0, tiled=True)

    dscores_local = (probs_local * (grads_local - row_dot)).astype(jnp.bfloat16)
    low_local = probs_local.astype(jnp.bfloat16)
    query_grads = (
        jnp.einsum(
            "bhxky,bkyhd->bxhd", dscores_local, local_keys, preferred_element_type=jnp.float32
        )
        + jnp.einsum(
            "bhxky,bkyhd->bxhd", dscores_rand, rand_keys, preferred_element_type=jnp.float32
        )
    ) * score_scale
    key_terms = (
        jnp.einsum(
            "bhxky,bxhd->bkyhd", dscores_local, query_blocks, preferred_element_type=jnp.float32
        )
        * score_scale
    )
    value_terms = jnp.einsum(
        "bhxky,bxhd->bkyhd", low_local, dout_blocks, preferred_element_type=jnp.float32
    )
    pair_terms = jnp.stack([key_terms, value_terms]).reshape(
        2, per_dev, local_count, BLOCK, features
    )
    framed_sum = jnp.pad(pair_terms[:, :, 0], ((0, 0), (0, 2), (0, 0), (0, 0)))
    framed_sum = framed_sum + jnp.pad(pair_terms[:, :, 1], ((0, 0), (1, 1), (0, 0), (0, 0)))
    framed_sum = framed_sum + jnp.pad(pair_terms[:, :, 2], ((0, 0), (2, 0), (0, 0), (0, 0)))
    totals = framed_sum[:, 1 : per_dev + 1]
    global_sum = jnp.sum(pair_terms[:, :, 3 : 3 + G], axis=1)
    rim_terms = jnp.concatenate([framed_sum[:, 0], framed_sum[:, -1]], axis=1)
    widened = extended_2(rim_terms.astype(jnp.bfloat16), (("seq", 1),), BLOCK).astype(
        rim_terms.dtype
    )
    totals = totals.at[:, 0].add(widened[:, :BLOCK])
    totals = totals.at[:, per_dev - 1].add(widened[:, -BLOCK:])
    everywhere = reduce_to_first(global_sum, "seq")
    padded_global = jnp.pad(everywhere, ((0, 0), (0, per_dev - G), (0, 0), (0, 0))) * (
        device == 0
    ).astype(jnp.float32)
    totals = totals + padded_global
    collected = jnp.einsum(
        "dcb,dcsxf->sbxf",
        chooser.astype(jnp.bfloat16),
        arrived.reshape(seq_count, capacity, 2, BLOCK, features),
        preferred_element_type=jnp.float32,
    )
    totals = totals + collected
    grad_rows = query_grads.reshape(tokens, features).astype(jnp.bfloat16)
    key_rows = totals[0].reshape(tokens, features).astype(jnp.bfloat16)
    value_rows = totals[1].reshape(tokens, features).astype(jnp.bfloat16)
    result = jnp.stack([grad_rows, key_rows, value_rows])
    result = lax.all_to_all(result, "head", split_axis=1, concat_axis=2, tiled=True)
    return (result[0], result[1], result[2])


def solution(mesh):
    in_specs = (
        P(("seq", "head"), None),
        P(("seq", "head"), None),
        P(("seq", "head"), None),
        P(("seq", "head"), None),
        P(),
    )
    out_specs = (P(("seq", "head"), None), P(("seq", "head"), None), P(("seq", "head"), None))
    return jax.shard_map(
        on_device, mesh=mesh, in_specs=in_specs, out_specs=out_specs, check_vma=False
    )
```

profile of v0, /device:TPU:64, one launch (start us, length us, event | category | flops | bytes accessed | tf_op | source)
XLA Modules:
  0.0 683.8 jit_solution(11837675565195276531)
XLA Ops:
  12.3 49.1 %all-to-all-done = bf16[4,160,2048]{1,0,2:T(4,128)(2,1)} async-done(((bf16[4,160,2048]{1,0,2:T(4,128)(2,1)}), bf16[4,160,2048]{1,0,2:T(4,128)(2,1)}, u32[]{:S(2)}, u32[]{:S(2)}) %all-to-all-start) | async-done | bytes 2621472 | tf_op jit(solution)/shard_map/all_to_all | solution.py:64
  61.5 7.4 %copy.402 = bf16[4,160,4,512]{3,2,1,0:T(4,128)(2,1)S(1)} copy(bf16[4,160,4,512]{1,0,3,2:T(4,128)(2,1)} %bitcast.6) | data formatting | bytes 5242880 | tf_op jit(solution)/shard_map/all_to_all | solution.py:64
  74.6 14.8 %collective-permute-done.1 = bf16[2,128,512]{2,1,0:T(8,128)(2,1)S(1)} collective-permute-done((bf16[2,128,512]{2,1,0:T(8,128)(2,1)S(1)}, bf16[2,128,512]{2,1,0:T(8,128)(2,1)S(1)}, u32[]{:S(2)}, u32[]{:S(2)}) %collective-permute-start.1) | collective-permute-done | bytes 262176 | tf_op jit(solution)/shard_map/ppermute | solution.py:23
  93.1 5.8 collective-permute-start.7
  118.7 11.3 %copy.358 = bf16[64,2,64,512]{3,2,1,0:T(8,128)(2,1)} copy(bf16[64,2,64,512]{3,0,2,1:T(8,128)(2,1)} %convolution_convert_fusion.1) | data formatting | bytes 16777216 | tf_op jit(solution)/shard_map/optimization_barrier | solution.py:100
  130.1 14.0 %all-to-all-start.1 = ((bf16[64,2,64,512]{3,2,1,0:T(8,128)(2,1)}), bf16[64,2,64,512]{3,2,1,0:T(8,128)(2,1)}, u32[]{:S(2)}, u32[]{:S(2)}) async-start(bf16[64,2,64,512]{3,2,1,0:T(8,128)(2,1)} %copy.358), calls=%async_computation.1 | async-start | bytes 16777216 | tf_op jit(solution)/shard_map/all_to_all | solution.py:101
  171.1 7.1 %reshape_squeeze.24 = bf16[10,5,64,4,128]{4,3,2,1,0:T(4,128)(2,1)} reshape(bf16[1,10,5,64,512]{4,3,2,1,0:T(8,128)(2,1)} %get-tuple-element.44) | data formatting | bytes 6553600 | tf_op jit(solution)/shard_map/reshape;squeeze | solution.py:113
  188.9 139.1 %all-to-all-done.1 = bf16[64,2,64,512]{3,2,1,0:T(8,128)(2,1)} async-done(((bf16[64,2,64,512]{3,2,1,0:T(8,128)(2,1)}), bf16[64,2,64,512]{3,2,1,0:T(8,128)(2,1)}, u32[]{:S(2)}, u32[]{:S(2)}) %all-to-all-start.1) | async-done | bytes 8388640 | tf_op jit(solution)/shard_map/all_to_all | solution.py:101
  328.1 6.1 gather_fusion.1
  383.4 7.3 %convolution_convert_fusion = bf16[64,2,64,512]{3,0,2,1:T(8,128)(2,1)} fusion(bf16[1,30,64,512]{3,1,2,0:T(8,128)(2,1)} %reshape.462, bf16[1,30,64,512]{3,1,2,0:T(8,128)(2,1)S(1)} %reshape.461, s32[30]{0:T(128)S(1)} %clamp_add_fusion), kind=kOutput, calls=%fused_computation.11 | convolution fusion | flops 263718784 | bytes 12320888 | tf_op jit(solution)/shard_map/js,jkxf->skxf/dot_general | solution.py:179
  390.7 11.5 %copy.387 = bf16[64,2,64,512]{3,2,1,0:T(8,128)(2,1)} copy(bf16[64,2,64,512]{3,0,2,1:T(8,128)(2,1)} %convolution_convert_fusion) | data formatting | bytes 16777216 | tf_op jit(solution)/shard_map/convert_element_type | solution.py:181
  402.1 9.1 %all-to-all-start.2 = ((bf16[64,2,64,512]{3,2,1,0:T(8,128)(2,1)}), bf16[64,2,64,512]{3,2,1,0:T(8,128)(2,1)}, u32[]{:S(2)}, u32[]{:S(2)}) async-start(bf16[64,2,64,512]{3,2,1,0:T(8,128)(2,1)} %copy.387), calls=%async_computation.2 | async-start | bytes 16777216 | tf_op jit(solution)/shard_map/all_to_all | solution.py:182
  411.3 6.3 fusion.58
  418.5 8.8 %copy.404 = f32[10,5,64,4,128]{4,3,2,0,1:T(4,128)} copy(f32[10,5,64,4,128]{4,2,1,3,0:T(8,128)S(1)} %bitcast.196) | data formatting | bytes 13107200 | tf_op jit(solution)/shard_map/stack | solution.py:203
  427.3 8.6 %reshape.460 = f32[1,10,5,64,512]{4,3,0,1,2:T(8,128)} reshape(f32[10,5,64,4,128]{4,3,2,0,1:T(4,128)} %copy.404) | data formatting | bytes 13107200 | tf_op jit(solution)/shard_map/stack | solution.py:203
  438.8 8.8 %copy.403 = f32[10,5,64,4,128]{4,3,2,0,1:T(4,128)} copy(f32[10,5,64,4,128]{4,2,1,3,0:T(8,128)S(1)} %multiply_bitcast_fusion) | data formatting | bytes 13107200 | tf_op jit(solution)/shard_map/stack | solution.py:203
  447.6 8.5 %reshape.459 = f32[1,10,5,64,512]{4,3,0,1,2:T(8,128)} reshape(f32[10,5,64,4,128]{4,3,2,0,1:T(4,128)} %copy.403) | data formatting | bytes 13107200 | tf_op jit(solution)/shard_map/stack | solution.py:203
  475.0 10.9 %collective-permute-done.11 = f32[2,2,64,512]{3,1,2,0:T(2,128)S(1)} collective-permute-done((f32[2,2,64,512]{3,1,2,0:T(2,128)S(1)}, f32[2,2,64,512]{3,1,2,0:T(2,128)S(1)}, u32[]{:S(2)}, u32[]{:S(2)}) %collective-permute-start.11) | collective-permute-done | bytes 524320 | tf_op jit(solution)/shard_map/ppermute | solution.py:33
  492.6 14.9 %collective-permute-done.12 = f32[2,2,64,512]{3,1,2,0:T(2,128)} collective-permute-done((f32[2,2,64,512]{3,1,2,0:T(2,128)}, f32[2,2,64,512]{3,1,2,0:T(2,128)}, u32[]{:S(2)}, u32[]{:S(2)}) %collective-permute-start.12) | collective-permute-done | bytes 524320 | tf_op jit(solution)/shard_map/ppermute | solution.py:33
  514.4 84.6 %collective-permute-done.13 = f32[2,2,64,512]{3,1,2,0:T(2,128)S(1)} collective-permute-done((f32[2,2,64,512]{3,1,2,0:T(2,128)S(1)}, f32[2,2,64,512]{3,1,2,0:T(2,128)S(1)}, u32[]{:S(2)}, u32[]{:S(2)}) %collective-permute-start.13) | collective-permute-done | bytes 524320 | tf_op jit(solution)/shard_map/ppermute | solution.py:33
  606.1 6.0 collective-permute-start.9
  625.8 6.4 scatter-add.9
  633.8 9.6 %fusion.7 = bf16[2,10,64,512]{3,1,2,0:T(8,128)(2,1)S(1)} fusion(f32[2,10,64,512]{3,1,2,0:T(8,128)} %scatter-add.9, f32[2,2,64,512]{3,1,2,0:T(2,128)S(1)} %add.208, bf16[64,2,64,512]{3,2,1,0:T(8,128)(2,1)} %all-to-all-done.2, f32[]{:T(128)S(6)} %convert_element_type.118, bf16[64,10]{0,1:T(8,128)(2,1)S(1)} %fusion.37), kind=kOutput, calls=%fused_computation.20 | convolution fusion | flops 86507520 | bytes 12846340 | tf_op jit(solution)/shard_map/dcb,dcsxf->sbxf/dot_general | solution.py:222
  646.3 31.8 %all_to_all.40 = bf16[3,640,512]{2,0,1:T(4,128)(2,1)S(1)} all-to-all(bf16[3,640,512]{2,0,1:T(4,128)(2,1)S(1)} %copy.391), channel_id=1, replica_groups=mesh['seq'=64,'head'=4] {'head'}, dimensions={1} | all-to-all | bytes 3932160 | tf_op jit(solution)/shard_map/all_to_all | solution.py:233
  (190 shorter events, 194.0 us)
Async XLA Ops:
  7.5 54.0 %all-to-all-start = ((bf16[4,160,2048]{1,0,2:T(4,128)(2,1)}), bf16[4,160,2048]{1,0,2:T(4,128)(2,1)}, u32[]{:S(2)}, u32[]{:S(2)}) async-start(bf16[4,160,2048]{1,0,2:T(4,128)(2,1)} %copy.338), calls=%async_computation | async-start | bytes 8388608 | tf_op jit(solution)/shard_map/all_to_all | solution.py:64
  71.1 1.9 collective-permute-start
  73.1 16.4 %collective-permute-start.1 = (bf16[2,128,512]{2,1,0:T(8,128)(2,1)S(1)}, bf16[2,128,512]{2,1,0:T(8,128)(2,1)S(1)}, u32[]{:S(2)}, u32[]{:S(2)}) collective-permute-start(bf16[2,128,512]{2,1,0:T(8,128)(2,1)S(1)} %fusion.76), channel_id=1, source_target_pairs={{0,64},{128,192},{1,65},{129,193},{2,66},{130,194},{3,67},{131,195}} | collective-permute-start | bytes 786440 | tf_op jit(solution)/shard_map/ppermute | solution.py:23
  89.5 9.4 %collective-permute-start.2 = (bf16[2,128,512]{2,1,0:T(8,128)(2,1)S(1)}, bf16[2,128,512]{2,1,0:T(8,128)(2,1)S(1)}, u32[]{:S(2)}, u32[]{:S(2)}) collective-permute-start(bf16[2,128,512]{2,1,0:T(8,128)(2,1)S(1)} %fusion.77), channel_id=1, source_target_pairs={{0,32},{64,96},{128,160},{192,224},{1,33},{65,97},{129,161},{193,2... | collective-permute-start | bytes 786440 | tf_op jit(solution)/shard_map/ppermute | solution.py:23
  91.1 25.5 %collective-permute-start.6 = (bf16[2,64,512]{2,1,0:T(8,128)(2,1)S(1)}, bf16[2,64,512]{2,1,0:T(8,128)(2,1)S(1)}, u32[]{:S(2)}, u32[]{:S(2)}) collective-permute-start(bf16[2,64,512]{2,1,0:T(8,128)(2,1)S(1)} %get-tuple-element.64), channel_id=1, source_target_pairs={{0,4},{4,8},{8,12},{12,16},{16,20},{20,24},{24,28},{28,32},{32,36}... | collective-permute-start | bytes 393224 | tf_op jit(solution)/shard_map/ppermute | solution.py:45
  93.1 23.6 %collective-permute-start.7 = (bf16[2,64,512]{2,1,0:T(8,128)(2,1)S(1)}, bf16[2,64,512]{2,1,0:T(8,128)(2,1)S(1)}, u32[]{:S(2)}, u32[]{:S(2)}) collective-permute-start(bf16[2,64,512]{2,1,0:T(8,128)(2,1)S(1)} %get-tuple-element.65), channel_id=1, source_target_pairs={{4,0},{8,4},{12,8},{16,12},{20,16},{24,20},{28,24},{32,28},{36,32}... | collective-permute-start | bytes 393224 | tf_op jit(solution)/shard_map/ppermute | solution.py:46
  98.9 5.2 collective-permute-start.3
  104.2 5.2 collective-permute-start.4
  109.4 8.5 %collective-permute-start.5 = (bf16[2,128,512]{2,1,0:T(8,128)(2,1)S(1)}, bf16[2,128,512]{2,1,0:T(8,128)(2,1)S(1)}, u32[]{:S(2)}, u32[]{:S(2)}) collective-permute-start(bf16[2,128,512]{2,1,0:T(8,128)(2,1)S(1)} %add.187), channel_id=1, source_target_pairs={{0,4},{8,12},{16,20},{24,28},{32,36},{40,44},{48,52},{56,60},{64,6... | collective-permute-start | bytes 786440 | tf_op jit(solution)/shard_map/ppermute | solution.py:23
  130.1 198.0 %all-to-all-start.1 = ((bf16[64,2,64,512]{3,2,1,0:T(8,128)(2,1)}), bf16[64,2,64,512]{3,2,1,0:T(8,128)(2,1)}, u32[]{:S(2)}, u32[]{:S(2)}) async-start(bf16[64,2,64,512]{3,2,1,0:T(8,128)(2,1)} %copy.358), calls=%async_computation.1 | async-start | bytes 16777216 | tf_op jit(solution)/shard_map/all_to_all | solution.py:101
  402.1 231.6 %all-to-all-start.2 = ((bf16[64,2,64,512]{3,2,1,0:T(8,128)(2,1)}), bf16[64,2,64,512]{3,2,1,0:T(8,128)(2,1)}, u32[]{:S(2)}, u32[]{:S(2)}) async-start(bf16[64,2,64,512]{3,2,1,0:T(8,128)(2,1)} %copy.387), calls=%async_computation.2 | async-start | bytes 16777216 | tf_op jit(solution)/shard_map/all_to_all | solution.py:182
  411.2 6.3 copy-start.14
  463.4 4.7 copy-start.5
  469.2 3.8 collective-permute-start.10
  473.5 12.4 %collective-permute-start.11 = (f32[2,2,64,512]{3,1,2,0:T(2,128)S(1)}, f32[2,2,64,512]{3,1,2,0:T(2,128)S(1)}, u32[]{:S(2)}, u32[]{:S(2)}) collective-permute-start(f32[2,2,64,512]{3,1,2,0:T(2,128)S(1)} %copy_add_fusion.1), channel_id=1, source_target_pairs={{8,0},{24,16},{40,32},{56,48},{72,64},{88,80},{104,96},{120,112},{... | collective-permute-start | bytes 1572872 | tf_op jit(solution)/shard_map/ppermute | solution.py:33
  487.0 20.6 %collective-permute-start.12 = (f32[2,2,64,512]{3,1,2,0:T(2,128)}, f32[2,2,64,512]{3,1,2,0:T(2,128)}, u32[]{:S(2)}, u32[]{:S(2)}) collective-permute-start(f32[2,2,64,512]{3,1,2,0:T(2,128)} %add.204), channel_id=1, source_target_pairs={{16,0},{48,32},{80,64},{112,96},{144,128},{176,160},{208,192},{240... | collective-permute-start | bytes 1572872 | tf_op jit(solution)/shard_map/ppermute | solution.py:33
  509.0 90.0 %collective-permute-start.13 = (f32[2,2,64,512]{3,1,2,0:T(2,128)S(1)}, f32[2,2,64,512]{3,1,2,0:T(2,128)S(1)}, u32[]{:S(2)}, u32[]{:S(2)}) collective-permute-start(f32[2,2,64,512]{3,1,2,0:T(2,128)S(1)} %add.205), channel_id=1, source_target_pairs={{32,0},{96,64},{160,128},{224,192},{33,1},{97,65},{161,129},{225,1... | collective-permute-start | bytes 1572872 | tf_op jit(solution)/shard_map/ppermute | solution.py:33
  513.2 99.0 %copy-start.9 = (bf16[10,4,64,3,64]{2,4,3,1,0:T(8,128)(2,1)S(1)}, bf16[10,4,64,3,64]{2,4,3,1,0:T(8,128)(2,1)}, u32[]{:S(2)}) copy-start(bf16[10,4,64,3,64]{2,4,3,1,0:T(8,128)(2,1)} %copy-done.8) | copy-start | bytes 2949124
  513.2 99.0 %copy-start.11 = (bf16[10,3,64,4,128]{4,3,2,1,0:T(4,128)(2,1)S(1)}, bf16[10,3,64,4,128]{4,3,2,1,0:T(4,128)(2,1)}, u32[]{:S(2)}) copy-start(bf16[10,3,64,4,128]{4,3,2,1,0:T(4,128)(2,1)} %copy-done.10) | copy-start | bytes 5898244
  600.1 16.9 %collective-permute-start.14 = (f32[2,2,64,512]{3,1,2,0:T(2,128)}, f32[2,2,64,512]{3,1,2,0:T(2,128)}, u32[]{:S(2)}, u32[]{:S(2)}) collective-permute-start(f32[2,2,64,512]{3,1,2,0:T(2,128)} %add.206), channel_id=1, source_target_pairs={{64,0},{192,128},{65,1},{193,129},{66,2},{194,130},{67,3},{195,131}} | collective-permute-start | bytes 1572872 | tf_op jit(solution)/shard_map/ppermute | solution.py:33
  604.2 16.7 %collective-permute-start.8 = (bf16[2,64,512]{2,1,0:T(8,128)(2,1)S(1)}, bf16[2,64,512]{2,1,0:T(8,128)(2,1)S(1)}, u32[]{:S(2)}, u32[]{:S(2)}) collective-permute-start(bf16[2,64,512]{2,1,0:T(8,128)(2,1)S(1)} %get-tuple-element.60), channel_id=1, source_target_pairs={{0,4},{4,8},{8,12},{12,16},{16,20},{20,24},{24,28},{28,32},{32,36}... | collective-permute-start | bytes 393224 | tf_op jit(solution)/shard_map/ppermute | solution.py:45
  606.1 10.5 %copy-start.16 = (f32[2,12,64,512]{3,2,0,1:T(8,128)S(1)}, f32[2,12,64,512]{3,2,0,1:T(8,128)}, u32[]{:S(2)}) copy-start(f32[2,12,64,512]{3,2,0,1:T(8,128)} %get-tuple-element.34) | copy-start | bytes 9437188
  606.1 14.8 %collective-permute-start.9 = (bf16[2,64,512]{2,1,0:T(8,128)(2,1)S(1)}, bf16[2,64,512]{2,1,0:T(8,128)(2,1)}, u32[]{:S(2)}, u32[]{:S(2)}) collective-permute-start(bf16[2,64,512]{2,1,0:T(8,128)(2,1)S(1)} %get-tuple-element.61), channel_id=1, source_target_pairs={{4,0},{8,4},{12,8},{16,12},{20,16},{24,20},{28,24},{32,28},{36,32}... | collective-permute-start | bytes 393224 | tf_op jit(solution)/shard_map/ppermute | solution.py:46
  619.2 13.1 %collective-permute-start.15 = (f32[2,2,64,512]{3,1,2,0:T(2,128)}, f32[2,2,64,512]{3,1,2,0:T(2,128)}, u32[]{:S(2)}, u32[]{:S(2)}) collective-permute-start(f32[2,2,64,512]{3,1,2,0:T(2,128)} %add.207), channel_id=1, source_target_pairs={{128,0},{129,1},{130,2},{131,3}} | collective-permute-start | bytes 1572872 | tf_op jit(solution)/shard_map/ppermute | solution.py:33
  (15 other events, 39.0 us)
where the time goes:
time: 690 us; the launch traced here: 684 us
  waiting for transfers between devices  323 us (47%)
  local copies, waits for them, and re-layouts  185 us (27%)
  starting transfers between devices  62.2 us (9%)
  other arithmetic  43.3 us (6%)
  matrix products  36.6 us (5%)
  blocking collectives  31.8 us (5%)
    all_to_all x1, waiting for transfers between devices, on_device(): lax.all_to_all(outgoing, 'seq', split_axis=0, concat_axis=0, tiled=True)  139 us
    ppermute x6, waiting for transfers between devices, reduce_to_first(): block = block + lax.ppermute(block, axis, pairs)  113 us
    all_to_all x1, waiting for transfers between devices, on_device(): lax.all_to_all(stacked, 'head', split_axis=2, concat_axis=1, tiled=True)  49.1 us
    another operation x5, local copies, waits for them, and re-layouts, on_device(): jnp.stack([key_terms, value_terms])  38.4 us
    all_to_all x1, blocking collectives, on_device(): lax.all_to_all(result, 'head', split_axis=1, concat_axis=2, tiled=True)  31.8 us
    ppermute x6, waiting for transfers between devices, broadcast(): block = block + lax.ppermute(block, axis, pairs)  21.7 us
    unnamed x46, local copies, waits for them, and re-layouts  19.2 us
    all_to_all x1, starting transfers between devices, on_device(): lax.all_to_all(outgoing, 'seq', split_axis=0, concat_axis=0, tiled=True)  14 us
  transfers between devices with their start and end apart: 19, of which 9 were waited for; matrix products, arithmetic and copies ran while one was open for 20% of the time, Pallas kernels for 0%

commit v1 on v0

v1 whole, which is shorter than its diff:
```python
import jax
import jax.numpy as jnp
from jax import lax
from jax.sharding import PartitionSpec as P

HD = 128
BLOCK = 64
G = 2
R = 3


big_negative = -1e30


def broadcast(block, axis, source):
    peers = lax.axis_size(axis)
    block = jnp.where(lax.axis_index(axis) == source, block, jnp.zeros_like(block))
    inner = 8 if peers % 8 == 0 else 1
    if inner > 1 and source == 0:
        outer = peers // inner
        received = [
            lax.ppermute(block, axis, [(0, k * inner)]) for k in range(1, outer)
        ]
        for part in received:
            block = block + part
        received = [
            lax.ppermute(block, axis, [(z * inner, z * inner + k) for z in range(outer)])
            for k in range(1, inner)
        ]
        for part in received:
            block = block + part
        return block
    step = 1
    while step * 2 < peers:
        step *= 2
    while step >= 1:
        pairs = [(i, i + step) for i in range(0, peers, 2 * step) if i + step < peers]
        block = block + lax.ppermute(block, axis, pairs)
        step //= 2
    return block


def reduce_to_first(block, axis):
    peers = lax.axis_size(axis)
    step = 1
    while step < peers:
        pairs = [(i + step, i) for i in range(0, peers, 2 * step) if i + step < peers]
        block = block + lax.ppermute(block, axis, pairs)
        step *= 2
    return block


def extended_2(shard, sides, width):
    for axis, dim in sides:
        peers, length = (lax.axis_size(axis), shard.shape[dim])
        up = [(i, (i + 1) % peers) for i in range(peers - 1)]
        down = [(j, i) for i, j in up]
        last = lax.slice_in_dim(shard, length - width, length, axis=dim)
        leading = lax.slice_in_dim(shard, 0, width, axis=dim)
        before = lax.ppermute(last, axis, up)
        after = lax.ppermute(leading, axis, down)
        shard = jnp.concatenate([before, shard, after], axis=dim)
    return shard


def request_plan(requested, device, per_dev):
    wanted_row = requested[device]
    owners = wanted_row // per_dev
    within = wanted_row % per_dev
    usable = jnp.ones(wanted_row.shape, jnp.bool_)
    positions = jnp.arange(owners.shape[0])
    earlier = (owners[:, None] == owners[None, :]) & (positions[None, :] < positions[:, None])
    slot_rank = jnp.sum(earlier.astype(jnp.int32), axis=1)
    return (owners, within, slot_rank, usable)


def attend_chunk(queries, out_grads, own_pairs, outgoing, global_pairs, extended,
                 chooser, my_slot, my_usable, device, seq_count, capacity):
    tokens, features = queries.shape
    head_count = features // HD
    per_dev = tokens // BLOCK
    rand_count = per_dev * R
    score_scale = HD ** (-0.5)
    incoming = lax.all_to_all(outgoing, "seq", split_axis=0, concat_axis=0, tiled=True)

    left_pair = extended[:, :BLOCK]
    right_pair = extended[:, -BLOCK:]
    framed = jnp.concatenate([left_pair[:, None], own_pairs, right_pair[:, None]], axis=1)
    window = jnp.stack(
        [framed[:, 0:per_dev], framed[:, 1 : per_dev + 1], framed[:, 2 : per_dev + 2]], axis=2
    )
    global_slots = jnp.broadcast_to(global_pairs[:, None], (2, per_dev, G, BLOCK, features))
    local = jnp.concatenate([window, global_slots], axis=2)
    local_count = 3 + G
    local_keys = local[0].reshape(per_dev, local_count, BLOCK, head_count, HD)
    local_values = local[1].reshape(per_dev, local_count, BLOCK, head_count, HD)
    block_index = device * per_dev + jnp.arange(per_dev)
    glob_index = jnp.arange(G)
    intersections = jnp.abs(glob_index[None, :] - block_index[:, None]) <= 1
    live_local = jnp.concatenate(
        [
            (block_index >= 1)[:, None],
            jnp.ones((per_dev, 1), jnp.bool_),
            (block_index <= seq_count * per_dev - 2)[:, None],
            jnp.logical_not(intersections),
        ],
        axis=1,
    )
    query_blocks = queries.reshape(per_dev, BLOCK, head_count, HD)
    dout_blocks = out_grads.reshape(per_dev, BLOCK, head_count, HD)
    scores_local = (
        jnp.einsum("bxhd,bkyhd->bhxky", query_blocks, local_keys, preferred_element_type=jnp.float32)
        * score_scale
    )
    scores_local = jnp.where(live_local[:, None, None, :, None], scores_local, big_negative)
    grads_local = jnp.einsum(
        "bxhd,bkyhd->bhxky", dout_blocks, local_values, preferred_element_type=jnp.float32
    )
    max_local = jnp.max(scores_local, axis=(3, 4), keepdims=True)

    fetched = incoming[my_slot]
    randoms = fetched.reshape(per_dev, R, 2, BLOCK, features)
    rand_keys = randoms[:, :, 0].reshape(per_dev, R, BLOCK, head_count, HD)
    rand_values = randoms[:, :, 1].reshape(per_dev, R, BLOCK, head_count, HD)
    scores_rand = (
        jnp.einsum("bxhd,bkyhd->bhxky", query_blocks, rand_keys, preferred_element_type=jnp.float32)
        * score_scale
    )
    grads_rand = jnp.einsum(
        "bxhd,bkyhd->bhxky", dout_blocks, rand_values, preferred_element_type=jnp.float32
    )
    row_max = jnp.maximum(max_local, jnp.max(scores_rand, axis=(3, 4), keepdims=True))
    weights_local = jnp.exp(scores_local - row_max)
    weights_rand = jnp.exp(scores_rand - row_max)
    row_total = jnp.sum(weights_local, axis=(3, 4), keepdims=True) + jnp.sum(
        weights_rand, axis=(3, 4), keepdims=True
    )
    probs_local = weights_local / row_total
    probs_rand = weights_rand / row_total
    row_dot = jnp.sum(probs_local * grads_local, axis=(3, 4), keepdims=True) + jnp.sum(
        probs_rand * grads_rand, axis=(3, 4), keepdims=True
    )
    dscores_rand = (probs_rand * (grads_rand - row_dot)).astype(jnp.bfloat16)
    low_rand = probs_rand.astype(jnp.bfloat16)
    key_rand = (
        jnp.einsum(
            "bhxky,bxhd->bkyhd", dscores_rand, query_blocks, preferred_element_type=jnp.float32
        )
        * score_scale
    )
    value_rand = jnp.einsum(
        "bhxky,bxhd->bkyhd", low_rand, dout_blocks, preferred_element_type=jnp.float32
    )
    rand_terms = (
        jnp.stack([key_rand, value_rand])
        .reshape(2, rand_count, BLOCK, features)
        .transpose(1, 0, 2, 3)
        .astype(jnp.bfloat16)
    )
    target = jnp.where(my_usable, my_slot, seq_count * capacity)
    placer = (target[:, None] == jnp.arange(seq_count * capacity)[None, :]).astype(jnp.bfloat16)
    outgoing_back = jnp.einsum(
        "js,jkxf->skxf", placer, rand_terms, preferred_element_type=jnp.float32
    ).astype(jnp.bfloat16)
    arrived = lax.all_to_all(outgoing_back, "seq", split_axis=0, concat_axis=0, tiled=True)

    dscores_local = (probs_local * (grads_local - row_dot)).astype(jnp.bfloat16)
    low_local = probs_local.astype(jnp.bfloat16)
    query_grads = (
        jnp.einsum(
            "bhxky,bkyhd->bxhd", dscores_local, local_keys, preferred_element_type=jnp.float32
        )
        + jnp.einsum(
            "bhxky,bkyhd->bxhd", dscores_rand, rand_keys, preferred_element_type=jnp.float32
        )
    ) * score_scale
    key_terms = (
        jnp.einsum(
            "bhxky,bxhd->bkyhd", dscores_local, query_blocks, preferred_element_type=jnp.float32
        )
        * score_scale
    )
    value_terms = jnp.einsum(
        "bhxky,bxhd->bkyhd", low_local, dout_blocks, preferred_element_type=jnp.float32
    )
    pair_terms = jnp.stack([key_terms, value_terms]).reshape(
        2, per_dev, local_count, BLOCK, features
    )
    framed_sum = jnp.pad(pair_terms[:, :, 0], ((0, 0), (0, 2), (0, 0), (0, 0)))
    framed_sum = framed_sum + jnp.pad(pair_terms[:, :, 1], ((0, 0), (1, 1), (0, 0), (0, 0)))
    framed_sum = framed_sum + jnp.pad(pair_terms[:, :, 2], ((0, 0), (2, 0), (0, 0), (0, 0)))
    totals = framed_sum[:, 1 : per_dev + 1]
    global_sum = jnp.sum(pair_terms[:, :, 3 : 3 + G], axis=1)
    rim_terms = jnp.concatenate([framed_sum[:, 0], framed_sum[:, -1]], axis=1)
    widened = extended_2(rim_terms.astype(jnp.bfloat16), (("seq", 1),), BLOCK).astype(
        rim_terms.dtype
    )
    totals = totals.at[:, 0].add(widened[:, :BLOCK])
    totals = totals.at[:, per_dev - 1].add(widened[:, -BLOCK:])
    everywhere = reduce_to_first(global_sum, "seq")
    padded_global = jnp.pad(everywhere, ((0, 0), (0, per_dev - G), (0, 0), (0, 0))) * (
        device == 0
    ).astype(jnp.float32)
    totals = totals + padded_global
    collected = jnp.einsum(
        "dcb,dcsxf->sbxf",
        chooser.astype(jnp.bfloat16),
        arrived.reshape(seq_count, capacity, 2, BLOCK, features),
        preferred_element_type=jnp.float32,
    )
    totals = totals + collected
    return query_grads.reshape(tokens, features), totals


def on_device(query, key, value, grad_out, rand_blocks):
    stacked = jnp.stack([query, key, value, grad_out])
    stacked = lax.all_to_all(stacked, "head", split_axis=2, concat_axis=1, tiled=True)
    queries, keys, values, out_grads = stacked[0], stacked[1], stacked[2], stacked[3]
    tokens, features = queries.shape
    head_count = features // HD
    per_dev = tokens // BLOCK
    seq_count = lax.axis_size("seq")
    device = lax.axis_index("seq")
    capacity = (per_dev * R + seq_count - 3) // (seq_count - 2)
    rand_count = per_dev * R
    score_scale = HD ** (-0.5)
    requested = rand_blocks.reshape(seq_count, rand_count)
    owners_all, within_all, rank_all, usable_all = jax.vmap(
        lambda sender: request_plan(requested, sender, per_dev)
    )(jnp.arange(seq_count, dtype=jnp.int32))
    to_me = usable_all & (owners_all == device)
    slot_ids = jnp.arange(capacity)
    block_ids = jnp.arange(per_dev)
    matches = (
        to_me[:, :, None, None]
        & (rank_all[:, :, None, None] == slot_ids[None, None, :, None])
        & (within_all[:, :, None, None] == block_ids[None, None, None, :])
    )
    chooser = jnp.sum(matches.astype(jnp.float32), axis=1)
    my_owners, my_within, my_rank, my_usable = request_plan(requested, device, per_dev)
    my_slot = jnp.clip(my_owners, 0, seq_count - 1) * capacity + my_rank
    own_pairs = jnp.stack([keys, values]).reshape(2, per_dev, BLOCK, features)
    served = jnp.einsum(
        "dcb,sbxf->dcsxf",
        chooser.astype(jnp.bfloat16),
        own_pairs,
        preferred_element_type=jnp.float32,
    ).astype(jnp.bfloat16)
    outgoing = served.reshape(seq_count * capacity, 2, BLOCK, features)
    leading = jnp.stack([keys[: G * BLOCK], values[: G * BLOCK]])
    global_pairs = broadcast(leading, "seq", 0).reshape(2, G, BLOCK, features)
    extended = extended_2(jnp.stack([keys, values]), (("seq", 1),), BLOCK)
    outgoing, global_pairs, extended = lax.optimization_barrier((outgoing, global_pairs, extended))
    chunk_heads = 2 if head_count % 2 == 0 else 1
    chunk_width = chunk_heads * HD
    pieces = []
    for c0 in range(0, features, chunk_width):
        pieces.append(
            attend_chunk(
                queries[:, c0 : c0 + chunk_width],
                out_grads[:, c0 : c0 + chunk_width],
                own_pairs[..., c0 : c0 + chunk_width],
                outgoing[..., c0 : c0 + chunk_width],
                global_pairs[..., c0 : c0 + chunk_width],
                extended[..., c0 : c0 + chunk_width],
                chooser, my_slot, my_usable, device, seq_count, capacity,
            )
        )
    query_grads = jnp.concatenate([p[0] for p in pieces], axis=-1)
    totals = jnp.concatenate([p[1] for p in pieces], axis=-1)
    grad_rows = query_grads.reshape(tokens, features).astype(jnp.bfloat16)
    key_rows = totals[0].reshape(tokens, features).astype(jnp.bfloat16)
    value_rows = totals[1].reshape(tokens, features).astype(jnp.bfloat16)
    result = jnp.stack([grad_rows, key_rows, value_rows])
    result = lax.all_to_all(result, "head", split_axis=1, concat_axis=2, tiled=True)
    return (result[0], result[1], result[2])


def solution(mesh):
    in_specs = (
        P(("seq", "head"), None),
        P(("seq", "head"), None),
        P(("seq", "head"), None),
        P(("seq", "head"), None),
        P(),
    )
    out_specs = (P(("seq", "head"), None), P(("seq", "head"), None), P(("seq", "head"), None))
    return jax.shard_map(
        on_device, mesh=mesh, in_specs=in_specs, out_specs=out_specs, check_vma=False
    )
```

time: 690 us -> 628 us (0.910)
  the two profiles are of different devices: /device:TPU:64 before, /device:TPU:128 now
where the time goes in v1:
time: 628 us; the launch traced here: 621 us
  local copies, waits for them, and re-layouts  209 us (33%)
  waiting for transfers between devices  199 us (32%)
  starting transfers between devices  111 us (18%)
  other arithmetic  39.1 us (6%)
  matrix products  38.3 us (6%)
  blocking collectives  22 us (4%)
    all_to_all x2, waiting for transfers between devices, attend_chunk(): lax.all_to_all(outgoing, 'seq', split_axis=0, concat_axis=0, tiled=True)  90.3 us
    all_to_all x1, waiting for transfers between devices, on_device(): lax.all_to_all(stacked, 'head', split_axis=2, concat_axis=1, tiled=True)  47.7 us
    another operation x9, local copies, waits for them, and re-layouts, attend_chunk(): jnp.stack([key_terms, value_terms])  35.5 us
    all_to_all x2, waiting for transfers between devices, attend_chunk(): lax.all_to_all(outgoing_back, 'seq', split_axis=0, concat_axis=0, tiled=T...  33.7 us
    all_to_all x2, starting transfers between devices, attend_chunk(): lax.all_to_all(outgoing, 'seq', split_axis=0, concat_axis=0, tiled=True)  30.8 us
    another operation x8, local copies, waits for them, and re-layouts, attend_chunk(): jnp.stack([key_rand, value_rand]).reshape(2, rand_count, BLOCK, features)  22.6 us
    all_to_all x1, blocking collectives, on_device(): lax.all_to_all(result, 'head', split_axis=1, concat_axis=2, tiled=True)  22 us
    all_to_all x2, starting transfers between devices, attend_chunk(): lax.all_to_all(outgoing_back, 'seq', split_axis=0, concat_axis=0, tiled=T...  21 us
  transfers between devices with their start and end apart: 37, of which 12 were waited for; matrix products, arithmetic and copies ran while one was open for 38% of the time, Pallas kernels for 0%

profile of v1, /device:TPU:128, one launch (start us, length us, event | category | flops | bytes accessed | tf_op | source)
XLA Modules:
  0.0 621.3 jit_solution(17319889405297996904)
XLA Ops:
  2.6 4.9 copy.700
  7.5 5.0 all-to-all-start
  14.0 47.7 %all-to-all-done = bf16[4,160,2048]{1,0,2:T(4,128)(2,1)} async-done(((bf16[4,160,2048]{1,0,2:T(4,128)(2,1)}), bf16[4,160,2048]{1,0,2:T(4,128)(2,1)}, u32[]{:S(2)}, u32[]{:S(2)}) %all-to-all-start) | async-done | bytes 2621472 | tf_op jit(solution)/shard_map/all_to_all | solution.py:217
  61.7 7.4 %copy.802 = bf16[4,160,4,512]{3,2,1,0:T(4,128)(2,1)S(1)} copy(bf16[4,160,4,512]{1,0,3,2:T(4,128)(2,1)} %bitcast.6) | data formatting | bytes 5242880 | tf_op jit(solution)/shard_map/all_to_all | solution.py:217
  79.3 7.2 %collective-permute-done.3 = bf16[2,128,512]{2,1,0:T(8,128)(2,1)S(1)} collective-permute-done((bf16[2,128,512]{2,1,0:T(8,128)(2,1)S(1)}, bf16[2,128,512]{2,1,0:T(8,128)(2,1)S(1)}, u32[]{:S(2)}, u32[]{:S(2)}) %collective-permute-start.3) | collective-permute-done | bytes 262176 | tf_op jit(solution)/shard_map/ppermute | solution.py:22
  111.0 20.4 %all-to-all-start.1 = ((bf16[64,2,64,256]{3,2,1,0:T(8,128)(2,1)}), bf16[64,2,64,256]{3,2,1,0:T(8,128)(2,1)}, u32[]{:S(2)}, u32[]{:S(2)}) async-start(bf16[64,2,64,256]{3,2,1,0:T(8,128)(2,1)} %copy.718), calls=%async_computation.1 | async-start | bytes 8388608 | tf_op jit(solution)/shard_map/all_to_all | solution.py:84
  139.3 6.6 %copy.738 = bf16[64,2,64,256]{3,2,1,0:T(8,128)(2,1)} copy(bf16[64,2,64,256]{3,0,2,1:T(8,128)(2,1)} %get-tuple-element.66) | data formatting | bytes 8388608 | tf_op jit(solution)/shard_map/slice | solution.py:263
  145.9 77.1 %all-to-all-done.1 = bf16[64,2,64,256]{3,2,1,0:T(8,128)(2,1)} async-done(((bf16[64,2,64,256]{3,2,1,0:T(8,128)(2,1)}), bf16[64,2,64,256]{3,2,1,0:T(8,128)(2,1)}, u32[]{:S(2)}, u32[]{:S(2)}) %all-to-all-start.1) | async-done | bytes 4194336 | tf_op jit(solution)/shard_map/all_to_all | solution.py:84
  223.0 10.3 %all-to-all-start.2 = ((bf16[64,2,64,256]{3,2,1,0:T(8,128)(2,1)}), bf16[64,2,64,256]{3,2,1,0:T(8,128)(2,1)}, u32[]{:S(2)}, u32[]{:S(2)}) async-start(bf16[64,2,64,256]{3,2,1,0:T(8,128)(2,1)} %copy.738), calls=%async_computation.2 | async-start | bytes 8388608 | tf_op jit(solution)/shard_map/all_to_all | solution.py:84
  311.8 13.1 %all-to-all-done.2 = bf16[64,2,64,256]{3,2,1,0:T(8,128)(2,1)} async-done(((bf16[64,2,64,256]{3,2,1,0:T(8,128)(2,1)}), bf16[64,2,64,256]{3,2,1,0:T(8,128)(2,1)}, u32[]{:S(2)}, u32[]{:S(2)}) %all-to-all-start.2) | async-done | bytes 4194336 | tf_op jit(solution)/shard_map/all_to_all | solution.py:84
  324.9 10.3 %all-to-all-start.3 = ((bf16[64,2,64,256]{3,2,1,0:T(8,128)(2,1)}), bf16[64,2,64,256]{3,2,1,0:T(8,128)(2,1)}, u32[]{:S(2)}, u32[]{:S(2)}) async-start(bf16[64,2,64,256]{3,2,1,0:T(8,128)(2,1)} %copy.766), calls=%async_computation.3 | async-start | bytes 8388608 | tf_op jit(solution)/shard_map/all_to_all | solution.py:165
  393.2 33.7 %all-to-all-done.3 = bf16[64,2,64,256]{3,2,1,0:T(8,128)(2,1)} async-done(((bf16[64,2,64,256]{3,2,1,0:T(8,128)(2,1)}), bf16[64,2,64,256]{3,2,1,0:T(8,128)(2,1)}, u32[]{:S(2)}, u32[]{:S(2)}) %all-to-all-start.3) | async-done | bytes 4194336 | tf_op jit(solution)/shard_map/all_to_all | solution.py:165
  426.8 10.7 %all-to-all-start.4 = ((bf16[64,2,64,256]{3,2,1,0:T(8,128)(2,1)}), bf16[64,2,64,256]{3,2,1,0:T(8,128)(2,1)}, u32[]{:S(2)}, u32[]{:S(2)}) async-start(bf16[64,2,64,256]{3,2,1,0:T(8,128)(2,1)} %copy.783), calls=%async_computation.4 | async-start | bytes 8388608 | tf_op jit(solution)/shard_map/all_to_all | solution.py:165
  437.5 6.4 %fusion.103 = (bf16[10,2,64,5,64]{2,4,3,1,0:T(8,128)(2,1)}, bf16[10,2,64,5,64]{2,4,3,1,0:T(8,128)(2,1)S(1)}, bf16[10,2,64,5,64]{2,4,3,1,0:T(8,128)(2,1)}, bf16[10,2,64,5,64]{2,4,3,1,0:T(8,128)(2,1)}) fusion(f32[10,2,64]{2,1,0:T(2,128)S(1)} %add.303, f32[10,2,64]{2,1,0:T(2,128)S(1)} %max.28, f32[10,2,64,5,64]{2,4,3,1,0:T(8,128)S(1)} %bitcast.289, ...), kind=kLoop, calls=%fused_computation.211 | loop fusion | flops 6553600 | bytes 9861170 | tf_op jit(solution)/shard_map/convert_element_type | solution.py:168
  461.0 5.6 reshape.632
  477.0 5.7 stack.119
  488.2 5.6 reshape.635
  507.3 5.7 collective-permute-start.17
  517.4 8.3 %collective-permute-done.19 = f32[2,2,64,256]{3,1,2,0:T(2,128)S(1)} collective-permute-done((f32[2,2,64,256]{3,1,2,0:T(2,128)S(1)}, f32[2,2,64,256]{3,1,2,0:T(2,128)S(1)}, u32[]{:S(2)}, u32[]{:S(2)}) %collective-permute-start.19) | collective-permute-done | bytes 262176 | tf_op jit(solution)/shard_map/ppermute | solution.py:48
  538.1 7.0 %collective-permute-start.25 = (bf16[2,64,256]{2,1,0:T(8,128)(2,1)S(1)}, bf16[2,64,256]{2,1,0:T(8,128)(2,1)S(1)}, u32[]{:S(2)}, u32[]{:S(2)}) collective-permute-start(bf16[2,64,256]{2,1,0:T(8,128)(2,1)S(1)} %copy-done.45), channel_id=1, source_target_pairs={{4,0},{8,4},{12,8},{16,12},{20,16},{24,20},{28,24},{32,28},{36,32}... | collective-permute-start | bytes 196616 | tf_op jit(solution)/shard_map/ppermute | solution.py:61
  559.0 4.8 collective-permute-done.22
  580.3 5.4 bitcast_add_fusion.1
  585.7 4.7 bitcast_add_fusion
  593.9 22.0 %all_to_all.50 = bf16[3,640,512]{2,0,1:T(4,128)(2,1)S(1)} all-to-all(bf16[3,640,512]{2,0,1:T(4,128)(2,1)S(1)} %copy.787), channel_id=1, replica_groups=mesh['seq'=64,'head'=4] {'head'}, dimensions={1} | all-to-all | bytes 3932160 | tf_op jit(solution)/shard_map/all_to_all | solution.py:275
  (368 shorter events, 283.1 us)
Async XLA Ops:
  7.5 54.2 %all-to-all-start = ((bf16[4,160,2048]{1,0,2:T(4,128)(2,1)}), bf16[4,160,2048]{1,0,2:T(4,128)(2,1)}, u32[]{:S(2)}, u32[]{:S(2)}) async-start(bf16[4,160,2048]{1,0,2:T(4,128)(2,1)} %copy.700), calls=%async_computation | async-start | bytes 8388608 | tf_op jit(solution)/shard_map/all_to_all | solution.py:217
  73.5 12.9 %collective-permute-start.3 = (bf16[2,128,512]{2,1,0:T(8,128)(2,1)S(1)}, bf16[2,128,512]{2,1,0:T(8,128)(2,1)S(1)}, u32[]{:S(2)}, u32[]{:S(2)}) collective-permute-start(bf16[2,128,512]{2,1,0:T(8,128)(2,1)S(1)} %maximum_select_fusion), channel_id=1, source_target_pairs={{0,128},{1,129},{2,130},{3,131}} | collective-permute-start | bytes 786440 | tf_op jit(solution)/shard_map/ppermute | solution.py:22
  74.8 13.5 %collective-permute-start.4 = (bf16[2,128,512]{2,1,0:T(8,128)(2,1)S(1)}, bf16[2,128,512]{2,1,0:T(8,128)(2,1)S(1)}, u32[]{:S(2)}, u32[]{:S(2)}) collective-permute-start(bf16[2,128,512]{2,1,0:T(8,128)(2,1)S(1)} %maximum_select_fusion), channel_id=1, source_target_pairs={{0,160},{1,161},{2,162},{3,163}} | collective-permute-start | bytes 786440 | tf_op jit(solution)/shard_map/ppermute | solution.py:22
  75.6 12.8 %collective-permute-start.5 = (bf16[2,128,512]{2,1,0:T(8,128)(2,1)S(1)}, bf16[2,128,512]{2,1,0:T(8,128)(2,1)S(1)}, u32[]{:S(2)}, u32[]{:S(2)}) collective-permute-start(bf16[2,128,512]{2,1,0:T(8,128)(2,1)S(1)} %maximum_select_fusion), channel_id=1, source_target_pairs={{0,192},{1,193},{2,194},{3,195}} | collective-permute-start | bytes 786440 | tf_op jit(solution)/shard_map/ppermute | solution.py:22
  76.3 12.1 %collective-permute-start.6 = (bf16[2,128,512]{2,1,0:T(8,128)(2,1)S(1)}, bf16[2,128,512]{2,1,0:T(8,128)(2,1)S(1)}, u32[]{:S(2)}, u32[]{:S(2)}) collective-permute-start(bf16[2,128,512]{2,1,0:T(8,128)(2,1)S(1)} %maximum_select_fusion), channel_id=1, source_target_pairs={{0,224},{1,225},{2,226},{3,227}} | collective-permute-start | bytes 786440 | tf_op jit(solution)/shard_map/ppermute | solution.py:22
  77.3 15.5 %collective-permute-start.14 = (bf16[2,64,512]{2,1,0:T(8,128)(2,1)S(1)}, bf16[2,64,512]{2,1,0:T(8,128)(2,1)S(1)}, u32[]{:S(2)}, u32[]{:S(2)}) collective-permute-start(bf16[2,64,512]{2,1,0:T(8,128)(2,1)S(1)} %get-tuple-element.107), channel_id=1, source_target_pairs={{0,4},{4,8},{8,12},{12,16},{16,20},{20,24},{24,28},{28,32},{32,36}... | collective-permute-start | bytes 393224 | tf_op jit(solution)/shard_map/ppermute | solution.py:60
  91.6 10.3 %collective-permute-start.12 = (bf16[2,128,512]{2,1,0:T(8,128)(2,1)S(1)}, bf16[2,128,512]{2,1,0:T(8,128)(2,1)S(1)}, u32[]{:S(2)}, u32[]{:S(2)}) collective-permute-start(bf16[2,128,512]{2,1,0:T(8,128)(2,1)S(1)} %add_add_fusion.1), channel_id=1, source_target_pairs={{0,24},{32,56},{64,88},{96,120},{128,152},{160,184},{192,216},{224... | collective-permute-start | bytes 786440 | tf_op jit(solution)/shard_map/ppermute | solution.py:27
  111.0 112.0 %all-to-all-start.1 = ((bf16[64,2,64,256]{3,2,1,0:T(8,128)(2,1)}), bf16[64,2,64,256]{3,2,1,0:T(8,128)(2,1)}, u32[]{:S(2)}, u32[]{:S(2)}) async-start(bf16[64,2,64,256]{3,2,1,0:T(8,128)(2,1)} %copy.718), calls=%async_computation.1 | async-start | bytes 8388608 | tf_op jit(solution)/shard_map/all_to_all | solution.py:84
  223.0 101.9 %all-to-all-start.2 = ((bf16[64,2,64,256]{3,2,1,0:T(8,128)(2,1)}), bf16[64,2,64,256]{3,2,1,0:T(8,128)(2,1)}, u32[]{:S(2)}, u32[]{:S(2)}) async-start(bf16[64,2,64,256]{3,2,1,0:T(8,128)(2,1)} %copy.738), calls=%async_computation.2 | async-start | bytes 8388608 | tf_op jit(solution)/shard_map/all_to_all | solution.py:84
  324.9 101.9 %all-to-all-start.3 = ((bf16[64,2,64,256]{3,2,1,0:T(8,128)(2,1)}), bf16[64,2,64,256]{3,2,1,0:T(8,128)(2,1)}, u32[]{:S(2)}, u32[]{:S(2)}) async-start(bf16[64,2,64,256]{3,2,1,0:T(8,128)(2,1)} %copy.766), calls=%async_computation.3 | async-start | bytes 8388608 | tf_op jit(solution)/shard_map/all_to_all | solution.py:165
  426.8 158.8 %all-to-all-start.4 = ((bf16[64,2,64,256]{3,2,1,0:T(8,128)(2,1)}), bf16[64,2,64,256]{3,2,1,0:T(8,128)(2,1)}, u32[]{:S(2)}, u32[]{:S(2)}) async-start(bf16[64,2,64,256]{3,2,1,0:T(8,128)(2,1)} %copy.783), calls=%async_computation.4 | async-start | bytes 8388608 | tf_op jit(solution)/shard_map/all_to_all | solution.py:165
  469.2 43.8 %collective-permute-start.18 = (f32[2,2,64,256]{3,1,2,0:T(2,128)S(1)}, f32[2,2,64,256]{3,1,2,0:T(2,128)S(1)}, u32[]{:S(2)}, u32[]{:S(2)}) collective-permute-start(f32[2,2,64,256]{3,1,2,0:T(2,128)S(1)} %copy.759), channel_id=1, source_target_pairs={{4,0},{12,8},{20,16},{28,24},{36,32},{44,40},{52,48},{60,56},{68,6... | collective-permute-start | bytes 786440 | tf_op jit(solution)/shard_map/ppermute | solution.py:48
  497.5 17.1 %collective-permute-start.26 = (f32[2,2,64,256]{3,1,2,0:T(2,128)S(1)}, f32[2,2,64,256]{3,1,2,0:T(2,128)S(1)}, u32[]{:S(2)}, u32[]{:S(2)}) collective-permute-start(f32[2,2,64,256]{3,1,2,0:T(2,128)S(1)} %copy.776), channel_id=1, source_target_pairs={{4,0},{12,8},{20,16},{28,24},{36,32},{44,40},{52,48},{60,56},{68,6... | collective-permute-start | bytes 786440 | tf_op jit(solution)/shard_map/ppermute | solution.py:48
  504.1 44.6 %collective-permute-start.16 = (bf16[2,64,256]{2,1,0:T(8,128)(2,1)S(1)}, bf16[2,64,256]{2,1,0:T(8,128)(2,1)}, u32[]{:S(2)}, u32[]{:S(2)}) collective-permute-start(bf16[2,64,256]{2,1,0:T(8,128)(2,1)S(1)} %get-tuple-element.113), channel_id=1, source_target_pairs={{0,4},{4,8},{8,12},{12,16},{16,20},{20,24},{24,28},{28,32},{32,36}... | collective-permute-start | bytes 196616 | tf_op jit(solution)/shard_map/ppermute | solution.py:60
  507.3 42.7 %collective-permute-start.17 = (bf16[2,64,256]{2,1,0:T(8,128)(2,1)}, bf16[2,64,256]{2,1,0:T(8,128)(2,1)}, u32[]{:S(2)}, u32[]{:S(2)}) collective-permute-start(bf16[2,64,256]{2,1,0:T(8,128)(2,1)} %get-tuple-element.114), channel_id=1, source_target_pairs={{4,0},{8,4},{12,8},{16,12},{20,16},{24,20},{28,24},{32,28},{36,32}... | collective-permute-start | bytes 196616 | tf_op jit(solution)/shard_map/ppermute | solution.py:61
  513.3 12.4 %collective-permute-start.19 = (f32[2,2,64,256]{3,1,2,0:T(2,128)S(1)}, f32[2,2,64,256]{3,1,2,0:T(2,128)S(1)}, u32[]{:S(2)}, u32[]{:S(2)}) collective-permute-start(f32[2,2,64,256]{3,1,2,0:T(2,128)S(1)} %copy_add_fusion.3), channel_id=1, source_target_pairs={{8,0},{24,16},{40,32},{56,48},{72,64},{88,80},{104,96},{120,112},{... | collective-permute-start | bytes 786440 | tf_op jit(solution)/shard_map/ppermute | solution.py:48
  514.9 13.7 %collective-permute-start.27 = (f32[2,2,64,256]{3,1,2,0:T(2,128)S(1)}, f32[2,2,64,256]{3,1,2,0:T(2,128)S(1)}, u32[]{:S(2)}, u32[]{:S(2)}) collective-permute-start(f32[2,2,64,256]{3,1,2,0:T(2,128)S(1)} %copy_add_fusion.2), channel_id=1, source_target_pairs={{8,0},{24,16},{40,32},{56,48},{72,64},{88,80},{104,96},{120,112},{... | collective-permute-start | bytes 786440 | tf_op jit(solution)/shard_map/ppermute | solution.py:48
  526.5 11.6 %collective-permute-start.20 = (f32[2,2,64,256]{3,1,2,0:T(2,128)}, f32[2,2,64,256]{3,1,2,0:T(2,128)}, u32[]{:S(2)}, u32[]{:S(2)}) collective-permute-start(f32[2,2,64,256]{3,1,2,0:T(2,128)} %add.314), channel_id=1, source_target_pairs={{16,0},{48,32},{80,64},{112,96},{144,128},{176,160},{208,192},{240... | collective-permute-start | bytes 786440 | tf_op jit(solution)/shard_map/ppermute | solution.py:48
  529.4 16.8 %collective-permute-start.28 = (f32[2,2,64,256]{3,1,2,0:T(2,128)}, f32[2,2,64,256]{3,1,2,0:T(2,128)}, u32[]{:S(2)}, u32[]{:S(2)}) collective-permute-start(f32[2,2,64,256]{3,1,2,0:T(2,128)} %add.327), channel_id=1, source_target_pairs={{16,0},{48,32},{80,64},{112,96},{144,128},{176,160},{208,192},{240... | collective-permute-start | bytes 786440 | tf_op jit(solution)/shard_map/ppermute | solution.py:48
  536.1 22.9 %collective-permute-start.24 = (bf16[2,64,256]{2,1,0:T(8,128)(2,1)S(1)}, bf16[2,64,256]{2,1,0:T(8,128)(2,1)S(1)}, u32[]{:S(2)}, u32[]{:S(2)}) collective-permute-start(bf16[2,64,256]{2,1,0:T(8,128)(2,1)S(1)} %copy-done.44), channel_id=1, source_target_pairs={{0,4},{4,8},{8,12},{12,16},{16,20},{20,24},{24,28},{28,32},{32,36}... | collective-permute-start | bytes 196616 | tf_op jit(solution)/shard_map/ppermute | solution.py:60
  538.1 20.9 %collective-permute-start.25 = (bf16[2,64,256]{2,1,0:T(8,128)(2,1)S(1)}, bf16[2,64,256]{2,1,0:T(8,128)(2,1)S(1)}, u32[]{:S(2)}, u32[]{:S(2)}) collective-permute-start(bf16[2,64,256]{2,1,0:T(8,128)(2,1)S(1)} %copy-done.45), channel_id=1, source_target_pairs={{4,0},{8,4},{12,8},{16,12},{20,16},{24,20},{28,24},{32,28},{36,32}... | collective-permute-start | bytes 196616 | tf_op jit(solution)/shard_map/ppermute | solution.py:61
  554.7 9.2 %collective-permute-start.22 = (f32[2,2,64,256]{3,1,2,0:T(2,128)S(1)}, f32[2,2,64,256]{3,1,2,0:T(2,128)S(1)}, u32[]{:S(2)}, u32[]{:S(2)}) collective-permute-start(f32[2,2,64,256]{3,1,2,0:T(2,128)S(1)} %add.316), channel_id=1, source_target_pairs={{64,0},{192,128},{65,1},{193,129},{66,2},{194,130},{67,3},{195,131}} | collective-permute-start | bytes 786440 | tf_op jit(solution)/shard_map/ppermute | solution.py:48
  564.0 14.1 %collective-permute-start.23 = (f32[2,2,64,256]{3,1,2,0:T(2,128)S(1)}, f32[2,2,64,256]{3,1,2,0:T(2,128)}, u32[]{:S(2)}, u32[]{:S(2)}) collective-permute-start(f32[2,2,64,256]{3,1,2,0:T(2,128)S(1)} %add.317), channel_id=1, source_target_pairs={{128,0},{129,1},{130,2},{131,3}} | collective-permute-start | bytes 786440 | tf_op jit(solution)/shard_map/ppermute | solution.py:48
  566.8 12.4 %collective-permute-start.31 = (f32[2,2,64,256]{3,1,2,0:T(2,128)S(1)}, f32[2,2,64,256]{3,1,2,0:T(2,128)}, u32[]{:S(2)}, u32[]{:S(2)}) collective-permute-start(f32[2,2,64,256]{3,1,2,0:T(2,128)S(1)} %add.330), channel_id=1, source_target_pairs={{128,0},{129,1},{130,2},{131,3}} | collective-permute-start | bytes 786440 | tf_op jit(solution)/shard_map/ppermute | solution.py:48
  (64 other events, 259.1 us)
